TPU v7x, 512 devices: a whole 4x4x16 slice. The times are simulated.
512 devices in a mesh: dp: 8 (over x, core), tensor: 64 (over z, y).
Axes of the slice: x: 4, y: 4, z: 16, core: 2. Of those that a mesh axis runs over, the one named last changes fastest.
Arguments:
- states: bfloat16 [65536, 2048], P(('dp', 'tensor')), may hold values from -150 to 150
- norm_gain: float32 [2048], replicated, may hold values from 0.1 to 1.9
- norm_bias: float32 [2048], replicated, may hold values from -3 to 3
- head_table: bfloat16 [250880, 2048], P('tensor', 'dp'), may hold values from -2 to 2
- seq_lengths: int32 [8], P('dp'), may hold values from 4096 to 8192
- scored_index: int32 [2048], P('dp'), may hold values from 0 to 8191
- targets: int32 [2048], P('dp'), may hold values from 0 to 250879
- slot_mask: int32 [2048], P('dp'), may hold values 0 or 1
Outputs:
- logprob: float32 [2048], P(('dp', 'tensor'))
- entropy: float32 [2048], P(('dp', 'tensor'))
All inputs are finite; a program needn't handle non-finite values. No bound on the sum of `slot_mask` on one device may be relied on, other than what follows from the above.
Results may differ from a plain program's by a relative error of at most 0.012.
The roundings to bfloat16 on the way count: a program that leaves them out, or rounds other values in their place, can miss the bound.
Values may be sent and summed in bfloat16 or wider, within the bound.
No kernel may reach another device: no remote copies, remote signals or barrier semaphores. Data moves between devices by JAX's collectives and lax.ppermute only.
A program may use at most 64 MiB of HBM per device.

v0:
```python
import jax
import jax.numpy as jnp
from jax import lax
from jax.sharding import Mesh, PartitionSpec as P

EPSILON = 1e-05
TENSOR = ("tz", "ty")


def layer_norm(states, norm_gain, norm_bias):
    values = states.astype(jnp.float32)
    center = jnp.mean(values, axis=1, keepdims=True)
    shifted = values - center
    variance = jnp.mean(shifted * shifted, axis=1, keepdims=True)
    return (shifted * lax.rsqrt(variance + EPSILON) * norm_gain + norm_bias).astype(jnp.bfloat16)


def contract_last(left, right):
    return lax.dot_general(
        left, right, (((1,), (1,)), ((), ())), preferred_element_type=jnp.float32
    )


def body(states, norm_gain, norm_bias, head_table, seq_lengths, scored_index, targets, slot_mask):
    local_rows = states.shape[0]
    devices = lax.axis_size(TENSOR)
    position = lax.axis_index(TENSOR)
    first_row = position * local_rows
    scored_count = scored_index.shape[0]
    owned_count = scored_count // devices
    offset = position * owned_count
    width = states.shape[1]
    row_iota = jnp.arange(local_rows, dtype=jnp.int32)
    picker = (scored_index[:, None] - first_row == row_iota[None, :]).astype(jnp.bfloat16)
    picked = jnp.dot(picker, states, preferred_element_type=jnp.float32).astype(jnp.bfloat16)
    ring = lax.axis_size("ty")
    by_y = picked.reshape(devices // ring, ring, owned_count, width).transpose(1, 0, 2, 3)
    near = lax.all_to_all(by_y, "ty", 0, 0, tiled=True)
    near = jnp.sum(near.astype(jnp.float32), axis=0).astype(jnp.bfloat16)
    arrived = lax.all_to_all(near, "tz", 0, 0, tiled=True)
    owned_rows = jnp.sum(arrived.astype(jnp.float32), axis=0)
    owned_normed = layer_norm(owned_rows, norm_gain, norm_bias)
    along_z = lax.all_to_all(
        jnp.broadcast_to(owned_normed[None], (devices // ring, owned_count, width)),
        "tz",
        0,
        0,
        tiled=True,
    )
    along_y = lax.all_to_all(
        jnp.broadcast_to(along_z[None], (ring, devices // ring, owned_count, width)),
        "ty",
        0,
        0,
        tiled=True,
    )
    chosen = along_y.transpose(1, 0, 2, 3).reshape(scored_count, width)
    vocab_local = head_table.shape[0]
    split = vocab_local // 32 * 16
    local_target = targets - position * vocab_local
    parts = []
    for low, high in ((0, split), (split, vocab_local)):
        logits = contract_last(
            chosen, lax.all_gather(head_table[low:high], "dp", axis=1, tiled=True)
        )
        vocab_iota = jnp.arange(low, high, dtype=jnp.int32)
        target_hits = local_target[:, None] == vocab_iota[None, :]
        part_maxima = jnp.max(logits, axis=1)
        shifted = logits - part_maxima[:, None]
        weights = jnp.exp(shifted)
        parts.append(
            jnp.stack(
                [
                    part_maxima,
                    jnp.sum(weights, axis=1),
                    jnp.sum(weights * shifted, axis=1),
                    jnp.sum(jnp.where(target_hits, logits, 0.0), axis=1),
                ],
                axis=1,
            )
        )
    stats = jnp.stack(parts, axis=1)
    gathered = lax.all_to_all(stats.reshape(devices, owned_count, 2, 4), TENSOR, 0, 0, tiled=True)
    gathered = gathered.transpose(0, 2, 1, 3).reshape(devices * 2, owned_count, 4)
    part_max = gathered[:, :, 0]
    maxima = jnp.max(part_max, axis=0)
    gap = part_max - maxima[None, :]
    scale = jnp.exp(gap)
    totals = jnp.sum(scale * gathered[:, :, 1], axis=0)
    weighted = jnp.sum(scale * (gathered[:, :, 2] + gap * gathered[:, :, 1]), axis=0)
    target_logit = jnp.sum(gathered[:, :, 3], axis=0)
    own_index = lax.dynamic_slice_in_dim(scored_index, offset, owned_count)
    own_mask = lax.dynamic_slice_in_dim(slot_mask, offset, owned_count)
    segment = local_rows * devices // seq_lengths.shape[0]
    sequence = own_index // segment
    seq_iota = jnp.arange(seq_lengths.shape[0], dtype=jnp.int32)
    length_of = jnp.sum(
        jnp.where(sequence[:, None] == seq_iota[None, :], seq_lengths[None, :], 0), axis=1
    )
    live_slot = (own_mask == 1) & (own_index % segment < length_of)
    log_total = jnp.log(totals)
    logprob = jnp.where(live_slot, target_logit - maxima - log_total, 0.0)
    entropy = jnp.where(live_slot, log_total - weighted / totals, 0.0)
    return (logprob, entropy)


def split_mesh(mesh):
    grid = mesh.devices
    first = grid[0]
    coords = [getattr(d, "coords", None) for d in first]
    ring = len({c[1] for c in coords}) if all((c is not None for c in coords)) else 1
    return Mesh(grid.reshape(grid.shape[0], grid.shape[1] // ring, ring), ("dp", "tz", "ty"))


def solution(mesh):
    return jax.shard_map(
        body,
        mesh=split_mesh(mesh),
        in_specs=(
            P(("dp", "tz", "ty"), None),
            P(),
            P(),
            P(("tz", "ty"), "dp"),
            P("dp"),
            P("dp"),
            P("dp"),
            P("dp"),
        ),
        out_specs=(P(("dp", "tz", "ty")), P(("dp", "tz", "ty"))),
        check_vma=False,
    )
```

profile of v0, /device:TPU:2, one launch (start us, length us, event | category | flops | bytes accessed | tf_op | source)
XLA Modules:
  0.0 195.1 jit_solution(13988544709984714789)
XLA Ops:
  7.2 2.4 %slice.19 = bf16[1952,256]{1,0:T(8,128)(2,1)} slice(bf16[3920,256]{1,0:T(8,128)(2,1)} %param.11), slice={[0:1952], [0:256]} | slice | bytes 1998848 | tf_op jit(solution)/shard_map/slice | solution.py:64
  9.7 1.0 slice.20
  10.8 0.5 convolution_convert_fusion
  12.2 19.4 %all_to_all.25 = bf16[4,16,4,2048]{3,2,1,0:T(4,128)(2,1)S(1)} all-to-all(bf16[4,16,4,2048]{3,2,1,0:T(4,128)(2,1)S(1)} %bitcast.15), channel_id=1, replica_groups=mesh['dp'=8,'tz'=16,'ty'=4] {'ty'}, dimensions={0} | all-to-all | bytes 2097152 | tf_op jit(solution)/shard_map/all_to_all | solution.py:38
  31.6 0.7 reduce_sum.124
  32.3 32.5 %all_to_all.26 = bf16[16,4,2048]{2,1,0:T(4,128)(2,1)S(1)} all-to-all(bf16[16,4,2048]{2,1,0:T(4,128)(2,1)S(1)} %reduce_sum.124), channel_id=1, replica_groups=mesh['dp'=8,'tz'=16,'ty'=4] {'tz'}, dimensions={0} | all-to-all | bytes 524288 | tf_op jit(solution)/shard_map/all_to_all | solution.py:40
  65.7 22.5 %all_to_all.27 = bf16[16,4,2048]{2,1,0:T(4,128)(2,1)S(1)} all-to-all(bf16[16,4,2048]{2,1,0:T(4,128)(2,1)S(1)} %broadcast_in_dim.26), channel_id=1, replica_groups=mesh['dp'=8,'tz'=16,'ty'=4] {'tz'}, dimensions={0} | all-to-all | bytes 524288 | tf_op jit(solution)/shard_map/all_to_all | solution.py:43
  88.2 1.5 broadcast_in_dim.27
  89.7 3.5 %all-to-all-start.3 = ((bf16[4,16,4,2048]{3,2,1,0:T(4,128)(2,1)}), bf16[4,16,4,2048]{3,2,1,0:T(4,128)(2,1)S(1)}, u32[]{:S(2)}, u32[]{:S(2)}) async-start(bf16[4,16,4,2048]{3,2,1,0:T(4,128)(2,1)} %broadcast_in_dim.27), calls=%async_computation.3 | async-start | bytes 2097152 | tf_op jit(solution)/shard_map/all_to_all | solution.py:50
  93.2 10.8 %all-to-all-done.3 = bf16[4,16,4,2048]{3,2,1,0:T(4,128)(2,1)S(1)} async-done(((bf16[4,16,4,2048]{3,2,1,0:T(4,128)(2,1)}), bf16[4,16,4,2048]{3,2,1,0:T(4,128)(2,1)S(1)}, u32[]{:S(2)}, u32[]{:S(2)}) %all-to-all-start.3) | async-done | bytes 1048608 | tf_op jit(solution)/shard_map/all_to_all | solution.py:50
  104.0 0.6 copy.56
  104.6 1.1 reshape.126
  105.7 6.0 %fusion.4 = (f32[256]{0:T(256)S(1)}, f32[256,1952]{0,1:T(8,128)S(1)}) fusion(bf16[256,2048]{1,0:T(8,128)(2,1)} %reshape.126, bf16[1952,2048]{1,0:T(8,128)(2,1)} %all-gather.3.cloned.1.call-done), kind=kOutput, calls=%fused_computation.40 | convolution fusion | flops 2047319808 | bytes 11043840 | tf_op jit(solution)/shard_map/dot_general | solution.py:19
  111.9 0.7 exponential_reduce_fusion.1
  113.2 24.7 %all-gather.5.cloned.1.call-done = bf16[1968,2048]{1,0:T(8,128)(2,1)} async-done(((bf16[1968,256]{1,0:T(8,128)(2,1)}), bf16[1968,2048]{1,0:T(8,128)(2,1)}) %all-gather.5.cloned.1.call-update) | async-done | bytes 8060944 | tf_op jit(solution)/shard_map/all_gather | solution.py:64
  137.9 6.1 %fusion.3 = (f32[256]{0:T(256)S(1)}, f32[256,1968]{0,1:T(8,128)S(1)}) fusion(bf16[256,2048]{1,0:T(8,128)(2,1)} %reshape.126, bf16[1968,2048]{1,0:T(8,128)(2,1)} %all-gather.5.cloned.1.call-done), kind=kOutput, calls=%fused_computation.39 | convolution fusion | flops 2064101120 | bytes 11125760 | tf_op jit(solution)/shard_map/dot_general | solution.py:19
  144.1 1.0 exponential_reduce_fusion
  145.8 0.9 copy.65
  146.7 15.6 %all-to-all-start.4 = ((f32[64,4,2,4]{1,3,2,0:T(4,128)}), f32[64,4,2,4]{1,3,2,0:T(4,128)S(1)}, u32[]{:S(2)}, u32[]{:S(2)}) async-start(f32[64,4,2,4]{1,3,2,0:T(4,128)} %copy.65), calls=%async_computation.4 | async-start | bytes 524288 | tf_op jit(solution)/shard_map/all_to_all | solution.py:83
  163.0 22.3 %all-to-all-done.4 = f32[64,4,2,4]{1,3,2,0:T(4,128)S(1)} async-done(((f32[64,4,2,4]{1,3,2,0:T(4,128)}), f32[64,4,2,4]{1,3,2,0:T(4,128)S(1)}, u32[]{:S(2)}, u32[]{:S(2)}) %all-to-all-start.4) | async-done | bytes 8224 | tf_op jit(solution)/shard_map/all_to_all | solution.py:83
  185.3 1.0 copy.66
  186.3 0.6 slice_reduce_fusion
  187.1 0.6 subtract_select_fusion
  187.7 0.5 subtract_select_fusion.1
  (48 shorter events, 3.5 us)
Async XLA Ops:
  7.2 3.7 %copy-start = (bf16[128,2048]{1,0:T(8,128)(2,1)S(1)}, bf16[128,2048]{1,0:T(8,128)(2,1)}, u32[]{:S(2)}) copy-start(bf16[128,2048]{1,0:T(8,128)(2,1)} %param.8) | copy-start | bytes 1572868
  7.2 2.5 %copy-start.1 = (bf16[3920,256]{1,0:T(8,128)(2,1)S(1)}, bf16[3920,256]{1,0:T(8,128)(2,1)}, u32[]{:S(2)}) copy-start(bf16[3920,256]{1,0:T(8,128)(2,1)} %param.11) | copy-start | bytes 6021124
  7.2 98.6 %all-gather.3.cloned.1.call-start = ((), (), s32[]{:S(2)}) async-start(), calls=%async_computation.5 | async-start | bytes 8994816 | tf_op jit(solution)/shard_map/all_gather | solution.py:64
  9.6 1.2 copy-start.4
  9.7 128.2 %all-gather.5.cloned.1.call-start = ((), (), s32[]{:S(2)}) async-start(), calls=%async_computation.6 | async-start | bytes 9068544 | tf_op jit(solution)/shard_map/all_gather | solution.py:64
  12.2 53.3 %copy-start.2 = (f32[2048]{0:T(1024)S(1)}, f32[2048]{0:T(1024)}, u32[]{:S(2)}) copy-start(f32[2048]{0:T(1024)} %param.10) | copy-start | bytes 24580
  12.2 53.3 %copy-start.3 = (f32[2048]{0:T(1024)S(1)}, f32[2048]{0:T(1024)}, u32[]{:S(2)}) copy-start(f32[2048]{0:T(1024)} %param.9) | copy-start | bytes 24580
  65.7 27.5 %copy-start.5 = (s32[256]{0:T(256)S(1)}, s32[256]{0:T(256)}, u32[]{:S(2)}) copy-start(s32[256]{0:T(256)} %param.14) | copy-start | bytes 3076
  89.7 14.4 %all-to-all-start.3 = ((bf16[4,16,4,2048]{3,2,1,0:T(4,128)(2,1)}), bf16[4,16,4,2048]{3,2,1,0:T(4,128)(2,1)S(1)}, u32[]{:S(2)}, u32[]{:S(2)}) async-start(bf16[4,16,4,2048]{3,2,1,0:T(4,128)(2,1)} %broadcast_in_dim.27), calls=%async_computation.3 | async-start | bytes 2097152 | tf_op jit(solution)/shard_map/all_to_all | solution.py:50
  144.1 43.1 %copy-start.6 = (s32[256]{0:T(256)S(1)}, s32[256]{0:T(256)}, u32[]{:S(2)}) copy-start(s32[256]{0:T(256)} %param.15) | copy-start | bytes 3076
  146.7 38.6 %all-to-all-start.4 = ((f32[64,4,2,4]{1,3,2,0:T(4,128)}), f32[64,4,2,4]{1,3,2,0:T(4,128)S(1)}, u32[]{:S(2)}, u32[]{:S(2)}) async-start(f32[64,4,2,4]{1,3,2,0:T(4,128)} %copy.65), calls=%async_computation.4 | async-start | bytes 524288 | tf_op jit(solution)/shard_map/all_to_all | solution.py:83
Sparse Core Ops, SparseCore 0:
  10.1 64.3 all-gather.2
  76.6 61.1 all-gather.4
where the time goes:
time: 196 us; the launch traced here: 195 us
  blocking collectives  74.4 us (38%)
  waiting for transfers between devices  57.8 us (29%)
  starting transfers between devices  19.2 us (10%)
  between operations  15 us (8%)
  matrix products  12.6 us (6%)
  local copies, waits for them, and re-layouts  11 us (6%)
  other arithmetic  5.14 us (3%)
    all_to_all x1, blocking collectives, body(): arrived = lax.all_to_all(near, 'tz', 0, 0, tiled=True)  32.5 us
    all_gather x2, waiting for transfers between devices, body(): lax.all_gather(head_table[low:high], 'dp', axis=1, tiled=True)  24.7 us
    all_to_all x1, blocking collectives, body(): lax.all_to_all(jnp.broadcast_to(owned_normed[None], (devices // ring, own...  22.5 us
    all_to_all x1, waiting for transfers between devices, body(): lax.all_to_all(stats.reshape(devices, owned_count, 2, 4), TENSOR, 0, 0, t...  22.3 us
    all_to_all x1, blocking collectives, body(): near = lax.all_to_all(by_y, 'ty', 0, 0, tiled=True)  19.4 us
    all_to_all x1, starting transfers between devices, body(): lax.all_to_all(stats.reshape(devices, owned_count, 2, 4), TENSOR, 0, 0, t...  15.6 us
    dot_general x2, matrix products, contract_last(): lax.dot_general(left, right, (((1,), (1,)), ((), ())), preferred_element_...  12.1 us
    all_to_all x1, waiting for transfers between devices, body(): lax.all_to_all(jnp.broadcast_to(along_z[None], (ring, devices // ring, ow...  10.8 us
  transfers between devices with their start and end apart: 4, of which 3 were waited for; matrix products, arithmetic and copies ran while one was open for 7% of the time, Pallas kernels for 0%

commit v1 on v0

--- a/solution.py
+++ b/solution.py
@@ -5,6 +5,27 @@
 
 EPSILON = 1e-05
 TENSOR = ("tz", "ty")
+
+
+def ring_gather(value, axis, dim):
+    size, index, rows = (lax.axis_size(axis), lax.axis_index(axis), value.shape[dim])
+    ahead = [(i, (i + 1) % size) for i in range(size)]
+    left = [(i, (i - 1) % size) for i in range(size)]
+    whole = jnp.zeros((*value.shape[:dim], size * rows, *value.shape[dim + 1 :]), value.dtype)
+    whole = lax.dynamic_update_slice_in_dim(whole, value, index * rows, axis=dim)
+    from_left = from_right = value
+    middle = size // 2
+    for step in range(1, middle + 1):
+        from_left = lax.ppermute(from_left, axis, ahead)
+        whole = lax.dynamic_update_slice_in_dim(
+            whole, from_left, (index - step) % size * rows, axis=dim
+        )
+        if step < size - middle:
+            from_right = lax.ppermute(from_right, axis, left)
+            whole = lax.dynamic_update_slice_in_dim(
+                whole, from_right, (index + step) % size * rows, axis=dim
+            )
+    return whole
 
 
 def layer_norm(states, norm_gain, norm_bias):
@@ -60,9 +81,7 @@
     local_target = targets - position * vocab_local
     parts = []
     for low, high in ((0, split), (split, vocab_local)):
-        logits = contract_last(
-            chosen, lax.all_gather(head_table[low:high], "dp", axis=1, tiled=True)
-        )
+        logits = contract_last(chosen, ring_gather(head_table[low:high], "dp", 1))
         vocab_iota = jnp.arange(low, high, dtype=jnp.int32)
         target_hits = local_target[:, None] == vocab_iota[None, :]
         part_maxima = jnp.max(logits, axis=1)

time: 196 us -> 171 us (0.87)
  the two profiles are of different devices: /device:TPU:2 before, /device:TPU:7 now
where the time goes in v1:
time: 171 us; the launch traced here: 170 us
  starting transfers between devices  66.5 us (39%)
  local copies, waits for them, and re-layouts  52.7 us (31%)
  waiting for transfers between devices  31.5 us (18%)
  matrix products  12.3 us (7%)
  other arithmetic  5.79 us (3%)
    ppermute x8, starting transfers between devices, ring_gather(): from_left = lax.ppermute(from_left, axis, ahead)  24.6 us
    all_to_all x1, waiting for transfers between devices, body(): lax.all_to_all(stats.reshape(devices, owned_count, 2, 4), TENSOR, 0, 0, t...  21.2 us
    dynamic_update_slice x8, local copies, waits for them, and re-layouts, ring_gather(): lax.dynamic_update_slice_in_dim(whole, from_left, (index - step) % size *...  18.6 us
    dynamic_update_slice x6, local copies, waits for them, and re-layouts, ring_gather(): lax.dynamic_update_slice_in_dim(whole, from_right, (index + step) % size...  12.7 us
    all_to_all x1, starting transfers between devices, body(): lax.all_to_all(stats.reshape(devices, owned_count, 2, 4), TENSOR, 0, 0, t...  12.5 us
    dot_general x2, matrix products, contract_last(): lax.dot_general(left, right, (((1,), (1,)), ((), ())), preferred_element_...  11.8 us
    all_to_all x1, starting transfers between devices, body(): lax.all_to_all(jnp.broadcast_to(owned_normed[None], (devices // ring, own...  11.7 us
    all_to_all x1, starting transfers between devices, body(): arrived = lax.all_to_all(near, 'tz', 0, 0, tiled=True)  10.4 us
  transfers between devices with their start and end apart: 19, of which 4 were waited for; matrix products, arithmetic and copies ran while one was open for 29% of the time, Pallas kernels for 0%

profile of v1, /device:TPU:7, one launch (start us, length us, event | category | flops | bytes accessed | tf_op | source)
XLA Modules:
  0.0 170.4 jit_solution(5661257417673574939)
XLA Ops:
  0.7 4.2 %broadcast_in_dim.32 = bf16[1952,2048]{1,0:T(8,128)(2,1)} broadcast(bf16[]{:T(256)} %constant.117.clone.1), dimensions={} | broadcast | bytes 7995394 | tf_op jit(solution)/shard_map/broadcast_in_dim | solution.py:14
  4.9 2.7 %fusion.3 = (bf16[1952,256]{1,0:T(8,128)(2,1)}, bf16[1952,2048]{1,0:T(8,128)(2,1)}) fusion(bf16[3920,256]{1,0:T(8,128)(2,1)} %param.11, bf16[1952,2048]{1,0:T(8,128)(2,1)} %broadcast_in_dim.32, s32[]{:T(128)S(6)} %select_n.116), kind=kLoop, calls=%fused_computation.55 | loop fusion | bytes 2998276 | tf_op jit(solution)/shard_map/slice | solution.py:84
  7.6 6.1 %collective-permute-start = (bf16[1952,256]{1,0:T(8,128)(2,1)}, bf16[1952,256]{1,0:T(8,128)(2,1)}, u32[]{:S(2)}, u32[]{:S(2)}) collective-permute-start(bf16[1952,256]{1,0:T(8,128)(2,1)} %get-tuple-element.19), channel_id=1, source_target_pairs={{0,64},{64,128},{128,192},{192,256},{256,320},{320,384},{384,448},... | collective-permute-start | bytes 2998280 | tf_op jit(solution)/shard_map/ppermute | solution.py:19
  16.2 3.5 %all-to-all-start = ((bf16[4,16,4,2048]{3,2,1,0:T(4,128)(2,1)}), bf16[4,16,4,2048]{3,2,1,0:T(4,128)(2,1)S(1)}, u32[]{:S(2)}, u32[]{:S(2)}) async-start(bf16[4,16,4,2048]{3,2,1,0:T(4,128)(2,1)} %bitcast.11), calls=%async_computation | async-start | bytes 2097152 | tf_op jit(solution)/shard_map/all_to_all | solution.py:59
  19.7 4.1 %broadcast_in_dim.64 = bf16[1968,2048]{1,0:T(8,128)(2,1)} broadcast(bf16[]{:T(256)} %constant.117.clone.1), dimensions={} | broadcast | bytes 8060930 | tf_op jit(solution)/shard_map/broadcast_in_dim | solution.py:14
  25.0 3.0 %collective-permute-start.7 = (bf16[1968,256]{1,0:T(8,128)(2,1)S(1)}, bf16[1968,256]{1,0:T(8,128)(2,1)}, u32[]{:S(2)}, u32[]{:S(2)}) collective-permute-start(bf16[1968,256]{1,0:T(8,128)(2,1)S(1)} %get-tuple-element.21), channel_id=1, source_target_pairs={{0,64},{64,128},{128,192},{192,256},{256,320},{320,384},{384,448},... | collective-permute-start | bytes 3022856 | tf_op jit(solution)/shard_map/ppermute | solution.py:19
  28.0 4.7 %all-to-all-done = bf16[4,16,4,2048]{3,2,1,0:T(4,128)(2,1)S(1)} async-done(((bf16[4,16,4,2048]{3,2,1,0:T(4,128)(2,1)}), bf16[4,16,4,2048]{3,2,1,0:T(4,128)(2,1)S(1)}, u32[]{:S(2)}, u32[]{:S(2)}) %all-to-all-start) | async-done | bytes 1048608 | tf_op jit(solution)/shard_map/all_to_all | solution.py:59
  34.1 10.4 %all-to-all-start.1 = ((bf16[16,4,2048]{2,1,0:T(4,128)(2,1)}), bf16[16,4,2048]{2,1,0:T(4,128)(2,1)S(1)}, u32[]{:S(2)}, u32[]{:S(2)}) async-start(bf16[16,4,2048]{2,1,0:T(4,128)(2,1)} %reduce_sum.124), calls=%async_computation.1 | async-start | bytes 524288 | tf_op jit(solution)/shard_map/all_to_all | solution.py:61
  44.5 4.3 %collective-permute-start.2 = (bf16[1952,256]{1,0:T(8,128)(2,1)}, bf16[1952,256]{1,0:T(8,128)(2,1)}, u32[]{:S(2)}, u32[]{:S(2)}) collective-permute-start(bf16[1952,256]{1,0:T(8,128)(2,1)} %collective-permute-done), channel_id=1, source_target_pairs={{0,64},{64,128},{128,192},{192,256},{256,320},{320,384},{384,448},... | collective-permute-start | bytes 2998280 | tf_op jit(solution)/shard_map/ppermute | solution.py:19
  53.4 3.0 %collective-permute-start.9 = (bf16[1968,256]{1,0:T(8,128)(2,1)}, bf16[1968,256]{1,0:T(8,128)(2,1)}, u32[]{:S(2)}, u32[]{:S(2)}) collective-permute-start(bf16[1968,256]{1,0:T(8,128)(2,1)} %collective-permute-done.7), channel_id=1, source_target_pairs={{0,64},{64,128},{128,192},{192,256},{256,320},{320,384},{384,448},... | collective-permute-start | bytes 3022856 | tf_op jit(solution)/shard_map/ppermute | solution.py:19
  56.4 2.4 %constant_dynamic-update-slice_fusion.6 = bf16[1968,2048]{1,0:T(8,128)(2,1)} fusion(bf16[1968,2048]{1,0:T(8,128)(2,1)} %get-tuple-element.22, bf16[1968,256]{1,0:T(8,128)(2,1)} %collective-permute-done.7, s32[]{:T(128)S(6)} %select_n.118), kind=kLoop, calls=%fused_computation.30 | loop fusion | bytes 2015236 | tf_op jit(solution)/shard_map/dynamic_update_slice | solution.py:20
  62.6 11.7 %all-to-all-start.2 = ((bf16[16,4,2048]{2,1,0:T(4,128)(2,1)}), bf16[16,4,2048]{2,1,0:T(4,128)(2,1)S(1)}, u32[]{:S(2)}, u32[]{:S(2)}) async-start(bf16[16,4,2048]{2,1,0:T(4,128)(2,1)} %broadcast_in_dim.30), calls=%async_computation.2 | async-start | bytes 524288 | tf_op jit(solution)/shard_map/all_to_all | solution.py:64
  74.3 3.2 %collective-permute-start.4 = (bf16[1952,256]{1,0:T(8,128)(2,1)}, bf16[1952,256]{1,0:T(8,128)(2,1)}, u32[]{:S(2)}, u32[]{:S(2)}) collective-permute-start(bf16[1952,256]{1,0:T(8,128)(2,1)} %collective-permute-done.2), channel_id=1, source_target_pairs={{0,64},{64,128},{128,192},{192,256},{256,320},{320,384},{384,448},... | collective-permute-start | bytes 2998280 | tf_op jit(solution)/shard_map/ppermute | solution.py:19
  79.8 2.9 %collective-permute-start.11 = (bf16[1968,256]{1,0:T(8,128)(2,1)}, bf16[1968,256]{1,0:T(8,128)(2,1)}, u32[]{:S(2)}, u32[]{:S(2)}) collective-permute-start(bf16[1968,256]{1,0:T(8,128)(2,1)} %collective-permute-done.9), channel_id=1, source_target_pairs={{0,64},{64,128},{128,192},{192,256},{256,320},{320,384},{384,448},... | collective-permute-start | bytes 3022856 | tf_op jit(solution)/shard_map/ppermute | solution.py:19
  88.5 3.0 %all-to-all-done.2 = bf16[16,4,2048]{2,1,0:T(4,128)(2,1)S(1)} async-done(((bf16[16,4,2048]{2,1,0:T(4,128)(2,1)}), bf16[16,4,2048]{2,1,0:T(4,128)(2,1)S(1)}, u32[]{:S(2)}, u32[]{:S(2)}) %all-to-all-start.2) | async-done | bytes 262176 | tf_op jit(solution)/shard_map/all_to_all | solution.py:64
  93.0 3.7 %all-to-all-start.3 = ((bf16[4,16,4,2048]{3,2,1,0:T(4,128)(2,1)}), bf16[4,16,4,2048]{3,2,1,0:T(4,128)(2,1)S(1)}, u32[]{:S(2)}, u32[]{:S(2)}) async-start(bf16[4,16,4,2048]{3,2,1,0:T(4,128)(2,1)} %broadcast_in_dim.31), calls=%async_computation.3 | async-start | bytes 2097152 | tf_op jit(solution)/shard_map/all_to_all | solution.py:71
  98.7 2.4 %constant_dynamic-update-slice_fusion.10 = bf16[1952,2048]{1,0:T(8,128)(2,1)} fusion(bf16[1952,2048]{1,0:T(8,128)(2,1)} %constant_dynamic-update-slice_fusion.11, bf16[1952,256]{1,0:T(8,128)(2,1)} %collective-permute-done.4, s32[]{:T(128)S(6)} %select_n.126), kind=kLoop, calls=%fused_computation.34 | loop fusion | bytes 1998852 | tf_op jit(solution)/shard_map/dynamic_update_slice | solution.py:20
  101.1 2.3 %constant_dynamic-update-slice_fusion.9 = bf16[1952,2048]{1,0:T(8,128)(2,1)} fusion(bf16[1952,2048]{1,0:T(8,128)(2,1)} %constant_dynamic-update-slice_fusion.10, bf16[1952,256]{1,0:T(8,128)(2,1)} %collective-permute-done.5, s32[]{:T(128)S(6)} %select_n.128), kind=kLoop, calls=%fused_computation.33 | loop fusion | bytes 1998852 | tf_op jit(solution)/shard_map/dynamic_update_slice | solution.py:25
  108.1 2.6 %all-to-all-done.3 = bf16[4,16,4,2048]{3,2,1,0:T(4,128)(2,1)S(1)} async-done(((bf16[4,16,4,2048]{3,2,1,0:T(4,128)(2,1)}), bf16[4,16,4,2048]{3,2,1,0:T(4,128)(2,1)S(1)}, u32[]{:S(2)}, u32[]{:S(2)}) %all-to-all-start.3) | async-done | bytes 1048608 | tf_op jit(solution)/shard_map/all_to_all | solution.py:71
  114.7 5.9 %fusion.6 = (f32[256]{0:T(256)S(1)}, f32[256,1952]{0,1:T(8,128)S(1)}) fusion(bf16[256,2048]{1,0:T(8,128)(2,1)} %reshape.126, bf16[1952,2048]{1,0:T(8,128)(2,1)} %constant_dynamic-update-slice_fusion.8), kind=kOutput, calls=%fused_computation.58 | convolution fusion | flops 2047319808 | bytes 11043840 | tf_op jit(solution)/shard_map/dot_general | solution.py:40
  122.0 2.4 %constant_dynamic-update-slice_fusion = bf16[1968,2048]{1,0:T(8,128)(2,1)} fusion(bf16[1968,2048]{1,0:T(8,128)(2,1)} %constant_dynamic-update-slice_fusion.1, bf16[1968,256]{1,0:T(8,128)(2,1)} %collective-permute-done.13, s32[]{:T(128)S(6)} %select_n.130), kind=kLoop, calls=%fused_computation.24 | loop fusion | bytes 2015236 | tf_op jit(solution)/shard_map/dynamic_update_slice | solution.py:20
  124.4 6.0 %fusion.5 = (f32[256]{0:T(256)S(1)}, f32[256,1968]{0,1:T(8,128)S(1)}) fusion(bf16[256,2048]{1,0:T(8,128)(2,1)} %reshape.126, bf16[1968,2048]{1,0:T(8,128)(2,1)} %constant_dynamic-update-slice_fusion), kind=kOutput, calls=%fused_computation.57 | convolution fusion | flops 2064101120 | bytes 11125760 | tf_op jit(solution)/shard_map/dot_general | solution.py:40
  133.0 12.5 %all-to-all-start.4 = ((f32[64,4,2,4]{1,3,2,0:T(4,128)}), f32[64,4,2,4]{1,3,2,0:T(4,128)S(1)}, u32[]{:S(2)}, u32[]{:S(2)}) async-start(f32[64,4,2,4]{1,3,2,0:T(4,128)} %copy.65), calls=%async_computation.4 | async-start | bytes 524288 | tf_op jit(solution)/shard_map/all_to_all | solution.py:102
  146.2 21.2 %all-to-all-done.4 = f32[64,4,2,4]{1,3,2,0:T(4,128)S(1)} async-done(((f32[64,4,2,4]{1,3,2,0:T(4,128)}), f32[64,4,2,4]{1,3,2,0:T(4,128)S(1)}, u32[]{:S(2)}, u32[]{:S(2)}) %all-to-all-start.4) | async-done | bytes 8224 | tf_op jit(solution)/shard_map/all_to_all | solution.py:102
  (89 shorter events, 40.7 us)
Async XLA Ops:
  0.6 13.1 %copy-start = (bf16[128,2048]{1,0:T(8,128)(2,1)S(1)}, bf16[128,2048]{1,0:T(8,128)(2,1)}, u32[]{:S(2)}) copy-start(bf16[128,2048]{1,0:T(8,128)(2,1)} %param.8) | copy-start | bytes 1572868
  7.6 36.9 %collective-permute-start = (bf16[1952,256]{1,0:T(8,128)(2,1)}, bf16[1952,256]{1,0:T(8,128)(2,1)}, u32[]{:S(2)}, u32[]{:S(2)}) collective-permute-start(bf16[1952,256]{1,0:T(8,128)(2,1)} %get-tuple-element.19), channel_id=1, source_target_pairs={{0,64},{64,128},{128,192},{192,256},{256,320},{320,384},{384,448},... | collective-permute-start | bytes 2998280 | tf_op jit(solution)/shard_map/ppermute | solution.py:19
  13.7 35.1 %collective-permute-start.1 = (bf16[1952,256]{1,0:T(8,128)(2,1)}, bf16[1952,256]{1,0:T(8,128)(2,1)}, u32[]{:S(2)}, u32[]{:S(2)}) collective-permute-start(bf16[1952,256]{1,0:T(8,128)(2,1)} %get-tuple-element.19), channel_id=1, source_target_pairs={{0,448},{64,0},{128,64},{192,128},{256,192},{320,256},{384,320},{4... | collective-permute-start | bytes 2998280 | tf_op jit(solution)/shard_map/ppermute | solution.py:24
  14.6 13.4 %copy-start.5 = (s32[256]{0:T(256)S(1)}, s32[256]{0:T(256)}, u32[]{:S(2)}) copy-start(s32[256]{0:T(256)} %param.14) | copy-start | bytes 3076
  16.2 16.6 %all-to-all-start = ((bf16[4,16,4,2048]{3,2,1,0:T(4,128)(2,1)}), bf16[4,16,4,2048]{3,2,1,0:T(4,128)(2,1)S(1)}, u32[]{:S(2)}, u32[]{:S(2)}) async-start(bf16[4,16,4,2048]{3,2,1,0:T(4,128)(2,1)} %bitcast.11), calls=%async_computation | async-start | bytes 2097152 | tf_op jit(solution)/shard_map/all_to_all | solution.py:59
  23.8 37.8 %copy-start.2 = (f32[2048]{0:T(1024)S(1)}, f32[2048]{0:T(1024)}, u32[]{:S(2)}) copy-start(f32[2048]{0:T(1024)} %param.10) | copy-start | bytes 24580
  23.8 37.8 %copy-start.3 = (f32[2048]{0:T(1024)S(1)}, f32[2048]{0:T(1024)}, u32[]{:S(2)}) copy-start(f32[2048]{0:T(1024)} %param.9) | copy-start | bytes 24580
  25.0 28.4 %collective-permute-start.7 = (bf16[1968,256]{1,0:T(8,128)(2,1)S(1)}, bf16[1968,256]{1,0:T(8,128)(2,1)}, u32[]{:S(2)}, u32[]{:S(2)}) collective-permute-start(bf16[1968,256]{1,0:T(8,128)(2,1)S(1)} %get-tuple-element.21), channel_id=1, source_target_pairs={{0,64},{64,128},{128,192},{192,256},{256,320},{320,384},{384,448},... | collective-permute-start | bytes 3022856 | tf_op jit(solution)/shard_map/ppermute | solution.py:19
  27.9 28.4 %collective-permute-start.8 = (bf16[1968,256]{1,0:T(8,128)(2,1)S(1)}, bf16[1968,256]{1,0:T(8,128)(2,1)}, u32[]{:S(2)}, u32[]{:S(2)}) collective-permute-start(bf16[1968,256]{1,0:T(8,128)(2,1)S(1)} %get-tuple-element.21), channel_id=1, source_target_pairs={{0,448},{64,0},{128,64},{192,128},{256,192},{320,256},{384,320},{4... | collective-permute-start | bytes 3022856 | tf_op jit(solution)/shard_map/ppermute | solution.py:24
  34.1 26.9 %all-to-all-start.1 = ((bf16[16,4,2048]{2,1,0:T(4,128)(2,1)}), bf16[16,4,2048]{2,1,0:T(4,128)(2,1)S(1)}, u32[]{:S(2)}, u32[]{:S(2)}) async-start(bf16[16,4,2048]{2,1,0:T(4,128)(2,1)} %reduce_sum.124), calls=%async_computation.1 | async-start | bytes 524288 | tf_op jit(solution)/shard_map/all_to_all | solution.py:61
  44.5 29.8 %collective-permute-start.2 = (bf16[1952,256]{1,0:T(8,128)(2,1)}, bf16[1952,256]{1,0:T(8,128)(2,1)}, u32[]{:S(2)}, u32[]{:S(2)}) collective-permute-start(bf16[1952,256]{1,0:T(8,128)(2,1)} %collective-permute-done), channel_id=1, source_target_pairs={{0,64},{64,128},{128,192},{192,256},{256,320},{320,384},{384,448},... | collective-permute-start | bytes 2998280 | tf_op jit(solution)/shard_map/ppermute | solution.py:19
  48.8 28.8 %collective-permute-start.3 = (bf16[1952,256]{1,0:T(8,128)(2,1)}, bf16[1952,256]{1,0:T(8,128)(2,1)}, u32[]{:S(2)}, u32[]{:S(2)}) collective-permute-start(bf16[1952,256]{1,0:T(8,128)(2,1)} %collective-permute-done.1), channel_id=1, source_target_pairs={{0,448},{64,0},{128,64},{192,128},{256,192},{320,256},{384,320},{4... | collective-permute-start | bytes 2998280 | tf_op jit(solution)/shard_map/ppermute | solution.py:24
  53.4 26.5 %collective-permute-start.9 = (bf16[1968,256]{1,0:T(8,128)(2,1)}, bf16[1968,256]{1,0:T(8,128)(2,1)}, u32[]{:S(2)}, u32[]{:S(2)}) collective-permute-start(bf16[1968,256]{1,0:T(8,128)(2,1)} %collective-permute-done.7), channel_id=1, source_target_pairs={{0,64},{64,128},{128,192},{192,256},{256,320},{320,384},{384,448},... | collective-permute-start | bytes 3022856 | tf_op jit(solution)/shard_map/ppermute | solution.py:19
  56.4 28.7 %collective-permute-start.10 = (bf16[1968,256]{1,0:T(8,128)(2,1)}, bf16[1968,256]{1,0:T(8,128)(2,1)S(1)}, u32[]{:S(2)}, u32[]{:S(2)}) collective-permute-start(bf16[1968,256]{1,0:T(8,128)(2,1)} %collective-permute-done.8), channel_id=1, source_target_pairs={{0,448},{64,0},{128,64},{192,128},{256,192},{320,256},{384,320},{4... | collective-permute-start | bytes 3022856 | tf_op jit(solution)/shard_map/ppermute | solution.py:24
  62.6 29.0 %all-to-all-start.2 = ((bf16[16,4,2048]{2,1,0:T(4,128)(2,1)}), bf16[16,4,2048]{2,1,0:T(4,128)(2,1)S(1)}, u32[]{:S(2)}, u32[]{:S(2)}) async-start(bf16[16,4,2048]{2,1,0:T(4,128)(2,1)} %broadcast_in_dim.30), calls=%async_computation.2 | async-start | bytes 524288 | tf_op jit(solution)/shard_map/all_to_all | solution.py:64
  74.3 22.4 %collective-permute-start.4 = (bf16[1952,256]{1,0:T(8,128)(2,1)}, bf16[1952,256]{1,0:T(8,128)(2,1)}, u32[]{:S(2)}, u32[]{:S(2)}) collective-permute-start(bf16[1952,256]{1,0:T(8,128)(2,1)} %collective-permute-done.2), channel_id=1, source_target_pairs={{0,64},{64,128},{128,192},{192,256},{256,320},{320,384},{384,448},... | collective-permute-start | bytes 2998280 | tf_op jit(solution)/shard_map/ppermute | solution.py:19
  77.5 23.6 %collective-permute-start.5 = (bf16[1952,256]{1,0:T(8,128)(2,1)}, bf16[1952,256]{1,0:T(8,128)(2,1)}, u32[]{:S(2)}, u32[]{:S(2)}) collective-permute-start(bf16[1952,256]{1,0:T(8,128)(2,1)} %collective-permute-done.3), channel_id=1, source_target_pairs={{0,448},{64,0},{128,64},{192,128},{256,192},{320,256},{384,320},{4... | collective-permute-start | bytes 2998280 | tf_op jit(solution)/shard_map/ppermute | solution.py:24
  79.8 23.6 %collective-permute-start.11 = (bf16[1968,256]{1,0:T(8,128)(2,1)}, bf16[1968,256]{1,0:T(8,128)(2,1)}, u32[]{:S(2)}, u32[]{:S(2)}) collective-permute-start(bf16[1968,256]{1,0:T(8,128)(2,1)} %collective-permute-done.9), channel_id=1, source_target_pairs={{0,64},{64,128},{128,192},{192,256},{256,320},{320,384},{384,448},... | collective-permute-start | bytes 3022856 | tf_op jit(solution)/shard_map/ppermute | solution.py:19
  85.1 20.8 %collective-permute-start.12 = (bf16[1968,256]{1,0:T(8,128)(2,1)S(1)}, bf16[1968,256]{1,0:T(8,128)(2,1)}, u32[]{:S(2)}, u32[]{:S(2)}) collective-permute-start(bf16[1968,256]{1,0:T(8,128)(2,1)S(1)} %collective-permute-done.10), channel_id=1, source_target_pairs={{0,448},{64,0},{128,64},{192,128},{256,192},{320,256},{384,320},{4... | collective-permute-start | bytes 3022856 | tf_op jit(solution)/shard_map/ppermute | solution.py:24
  93.0 17.7 %all-to-all-start.3 = ((bf16[4,16,4,2048]{3,2,1,0:T(4,128)(2,1)}), bf16[4,16,4,2048]{3,2,1,0:T(4,128)(2,1)S(1)}, u32[]{:S(2)}, u32[]{:S(2)}) async-start(bf16[4,16,4,2048]{3,2,1,0:T(4,128)(2,1)} %broadcast_in_dim.31), calls=%async_computation.3 | async-start | bytes 2097152 | tf_op jit(solution)/shard_map/all_to_all | solution.py:71
  96.7 15.7 %collective-permute-start.6 = (bf16[1952,256]{1,0:T(8,128)(2,1)}, bf16[1952,256]{1,0:T(8,128)(2,1)}, u32[]{:S(2)}, u32[]{:S(2)}) collective-permute-start(bf16[1952,256]{1,0:T(8,128)(2,1)} %collective-permute-done.4), channel_id=1, source_target_pairs={{0,64},{64,128},{128,192},{192,256},{256,320},{320,384},{384,448},... | collective-permute-start | bytes 2998280 | tf_op jit(solution)/shard_map/ppermute | solution.py:19
  103.5 18.6 %collective-permute-start.13 = (bf16[1968,256]{1,0:T(8,128)(2,1)}, bf16[1968,256]{1,0:T(8,128)(2,1)}, u32[]{:S(2)}, u32[]{:S(2)}) collective-permute-start(bf16[1968,256]{1,0:T(8,128)(2,1)} %collective-permute-done.11), channel_id=1, source_target_pairs={{0,64},{64,128},{128,192},{192,256},{256,320},{320,384},{384,448},... | collective-permute-start | bytes 3022856 | tf_op jit(solution)/shard_map/ppermute | solution.py:19
  124.4 44.9 %copy-start.6 = (s32[256]{0:T(256)S(1)}, s32[256]{0:T(256)}, u32[]{:S(2)}) copy-start(s32[256]{0:T(256)} %param.15) | copy-start | bytes 3076
  133.0 34.4 %all-to-all-start.4 = ((f32[64,4,2,4]{1,3,2,0:T(4,128)}), f32[64,4,2,4]{1,3,2,0:T(4,128)S(1)}, u32[]{:S(2)}, u32[]{:S(2)}) async-start(f32[64,4,2,4]{1,3,2,0:T(4,128)} %copy.65), calls=%async_computation.4 | async-start | bytes 524288 | tf_op jit(solution)/shard_map/all_to_all | solution.py:102
  (2 other events, 17.2 us)
